TPU v7x, 128 devices: a whole 4x4x4 slice. The times are simulated.
128 devices in a mesh: dp: 32 (over y, x, core), mp: 4 (over z).
Axes of the slice: x: 4, y: 4, z: 4, core: 2. Of those that a mesh axis runs over, the one named last changes fastest.
Arguments:
- hidden: bfloat16 [4096, 2560], P('dp', 'mp'), may hold values from -6 to 6
- norm_gain: bfloat16 [2560], replicated, may hold values from 0.5 to 1.5
- shared_gate: bfloat16 [2560, 3072], P(None, 'mp'), may hold values from -0.125 to 0.125
- shared_up: bfloat16 [2560, 3072], P(None, 'mp'), may hold values from -0.125 to 0.125
- shared_down: bfloat16 [3072, 2560], P('mp'), may hold values from -0.109375 to 0.109375
- expert_gate: bfloat16 [64, 2560, 1536], P('dp', None, 'mp'), may hold values from -0.125 to 0.125
- expert_up: bfloat16 [64, 2560, 1536], P('dp', None, 'mp'), may hold values from -0.125 to 0.125
- expert_down: bfloat16 [64, 1536, 2560], P('dp', 'mp'), may hold values from -0.15625 to 0.15625
- adapter_in: bfloat16 [64, 3072, 16], P('dp', 'mp'), may hold values from -0.109375 to 0.109375
- adapter_out: bfloat16 [64, 16, 2560], P('dp'), may hold values from -1.5 to 1.5
- active: int32 [16], replicated, may hold values from 0 to 63, as said below
- lengths: int32 [64], replicated, may hold values from 1 to 1024, 4096 in all
- request_adapter: int32 [64], replicated, may hold values from 0 to 15
- routes: int32 [4096, 6], P('dp'), may hold values from 0 to 63, all different within a row; in each aligned block of 128 rows (0 to 127, 128 to 255, ...) at most 16 rows name the same one
- route_weights: float32 [4096, 6], P('dp'), may hold values from 0.05 to 0.35
Outputs:
- layer_out: bfloat16 [4096, 2560], P('dp', 'mp')
Inputs may be any that keep to these rules, and one draw needn't show every extreme that they name: `active`: the entries are distinct. `routes`: within the 128 rows of one index of dp no expert is named more than 16 times, and that many is reached; a row names distinct experts.
All inputs are finite; a program needn't handle non-finite values.
Results may differ from a plain program's by a relative error of at most 0.015.
Values may be sent and summed in bfloat16 or wider, within the bound.
No kernel may reach another device: no remote copies, remote signals or barrier semaphores. Data moves between devices by JAX's collectives and lax.ppermute only.
A program may use at most 128 MiB of HBM per device.

v0:
```python
import jax
import jax.numpy as jnp
from jax import lax
from jax.sharding import PartitionSpec as P


def experts_apply(slots_in, expert_gate, expert_up, expert_down):
    gate_val = jnp.einsum(
        "sjcd,jdf->sjcf", slots_in, expert_gate, preferred_element_type=jnp.float32
    )
    up_val = jnp.einsum("sjcd,jdf->sjcf", slots_in, expert_up, preferred_element_type=jnp.float32)
    inner = (jax.nn.silu(gate_val) * up_val).astype(jnp.bfloat16)
    return jnp.einsum("sjcf,jfd->sjcd", inner, expert_down, preferred_element_type=jnp.float32)


def body(
    hidden,
    norm_gain,
    shared_gate,
    shared_up,
    shared_down,
    expert_gate,
    expert_up,
    expert_down,
    adapter_in,
    adapter_out,
    active,
    lengths,
    request_adapter,
    routes,
    route_weights,
):
    tok_rows = routes.shape[0]
    top_count = routes.shape[1]
    dp_count = lax.axis_size("dp")
    mp_count = lax.axis_size("mp")
    dp_index = lax.axis_index("dp")
    mp_index = lax.axis_index("mp")
    local_experts = expert_gate.shape[0]
    total_experts = local_experts * dp_count
    capacity = mp_count * max(1, tok_rows * top_count * 4 // (total_experts * mp_count * 3))
    col_width = hidden.shape[1]
    col_start = mp_index * col_width
    active_count = active.shape[0]
    rank_width = adapter_in.shape[2]
    local_adapters = adapter_in.shape[0]
    owned_ids = dp_index * local_adapters + jnp.arange(local_adapters, dtype=jnp.int32)
    selector = (active[:, None] == owned_ids[None, :]).astype(jnp.bfloat16)
    out_cols = lax.dynamic_slice_in_dim(adapter_out, col_start, col_width, axis=2)
    picked_in = jnp.einsum(
        "ji,isr->jsr", selector, adapter_in, preferred_element_type=jnp.float32
    ).astype(jnp.bfloat16)
    picked_out = jnp.einsum(
        "ji,ird->jrd", selector, out_cols, preferred_element_type=jnp.float32
    ).astype(jnp.bfloat16)
    picked_in, picked_out = lax.psum((picked_in, picked_out), "dp")
    gathered = lax.all_gather(hidden, "mp", axis=1, tiled=True)
    values = gathered.astype(jnp.float32)
    factor = lax.rsqrt(jnp.mean(values * values, axis=-1, keepdims=True) + 1e-06)
    normed = (values * factor * norm_gain.astype(jnp.float32)).astype(jnp.bfloat16)
    width = normed.shape[1]
    shared_lin = jnp.dot(normed, shared_gate, preferred_element_type=jnp.float32)
    shared_pre = jnp.dot(normed, shared_up, preferred_element_type=jnp.float32)
    shared_act = (jax.nn.silu(shared_lin) * shared_pre).astype(jnp.bfloat16)
    request_end = jnp.cumsum(lengths)
    positions = dp_index * tok_rows + jnp.arange(tok_rows, dtype=jnp.int32)
    request_of = jnp.sum((request_end[None, :] <= positions[:, None]).astype(jnp.int32), axis=1)
    request_hot = (
        request_of[:, None] == jnp.arange(lengths.shape[0], dtype=jnp.int32)[None, :]
    ).astype(jnp.int32)
    slot_of = jnp.sum(request_hot * request_adapter[None, :], axis=1)
    chosen = (slot_of[:, None] == jnp.arange(active_count, dtype=jnp.int32)[None, :]).astype(
        jnp.float32
    )
    in_matrix = jnp.transpose(picked_in, (1, 0, 2)).reshape(
        shared_act.shape[1], active_count * rank_width
    )
    lowrank = jnp.dot(shared_act, in_matrix, preferred_element_type=jnp.float32)
    lowrank_sel = jnp.sum(
        lowrank.reshape(tok_rows, active_count, rank_width) * chosen[:, :, None], axis=1
    )
    lowrank_sel = lax.psum(lowrank_sel, "mp")
    lowrank = (chosen[:, :, None] * lowrank_sel[:, None, :]).reshape(
        tok_rows, active_count * rank_width
    )
    adapted = jnp.dot(
        lowrank,
        picked_out.reshape(active_count * rank_width, col_width).astype(jnp.float32),
        precision=lax.Precision.HIGHEST,
    )
    flat_routes = routes.reshape(-1)
    expert_hot = (
        flat_routes[:, None] == jnp.arange(total_experts, dtype=jnp.int32)[None, :]
    ).astype(jnp.int32)
    earlier = jnp.cumsum(expert_hot, axis=0) - expert_hot
    position = jnp.sum(earlier * expert_hot, axis=1)
    slot_index = (flat_routes * capacity + position).reshape(tok_rows, top_count)
    slot_count = total_experts * capacity
    slot_hit = slot_index[:, :, None] == jnp.arange(slot_count, dtype=jnp.int32)[None, None, :]
    dispatch = jnp.any(slot_hit, axis=1).astype(jnp.bfloat16)
    send_rows = jnp.einsum(
        "ts,td->sd", dispatch, normed, preferred_element_type=jnp.float32
    ).astype(jnp.bfloat16)
    send_rows = send_rows.reshape(dp_count, local_experts, capacity, width)
    returned = lax.all_to_all(
        experts_apply(
            lax.all_to_all(send_rows, "dp", split_axis=0, concat_axis=0, tiled=True),
            expert_gate,
            expert_up,
            expert_down,
        ).astype(jnp.bfloat16),
        "dp",
        split_axis=0,
        concat_axis=0,
        tiled=True,
    )
    returned = returned.reshape(slot_count, width)
    combine = jnp.sum(jnp.where(slot_hit, route_weights[:, :, None], 0.0), axis=1)
    combine_hi = combine.astype(jnp.bfloat16)
    combine_lo = (combine - combine_hi.astype(jnp.float32)).astype(jnp.bfloat16)
    routed = jnp.dot(combine_hi, returned, preferred_element_type=jnp.float32) + jnp.dot(
        combine_lo, returned, preferred_element_type=jnp.float32
    )
    partial_out = jnp.dot(shared_act, shared_down, preferred_element_type=jnp.float32) + routed
    own_cols = lax.dynamic_slice_in_dim(partial_out, col_start, col_width, axis=1) + adapted
    partial_out = lax.dynamic_update_slice_in_dim(partial_out, own_cols, col_start, axis=1)
    return lax.psum_scatter(partial_out.astype(jnp.bfloat16), "mp", scatter_dimension=1, tiled=True)


def solution(mesh):
    in_specs = (
        P("dp", "mp"),
        P(),
        P(None, "mp"),
        P(None, "mp"),
        P("mp", None),
        P("dp", None, "mp"),
        P("dp", None, "mp"),
        P("dp", "mp", None),
        P("dp", "mp", None),
        P("dp", None, None),
        P(),
        P(),
        P(),
        P("dp", None),
        P("dp", None),
    )
    out_specs = P("dp", "mp")
    return jax.shard_map(body, mesh=mesh, in_specs=in_specs, out_specs=out_specs, check_vma=False)
```

profile of v0, /device:TPU:0, one launch (start us, length us, event | category | flops | bytes accessed | tf_op | source)
XLA Modules:
  0.0 315.9 jit_solution(4285871344129331172)
XLA Ops:
  6.5 0.0 copy-start
  6.5 0.8 copy.60
  7.4 0.1 eq.85
  7.5 0.1 eq.81
  7.7 1.8 reduce-window.18
  9.5 0.3 slice_reduce_fusion
  9.8 0.1 fusion.34
  9.9 0.1 reduce_sum.58
  10.1 0.1 copy.63
  10.1 0.7 multiply_add_fusion
  10.8 0.5 fusion.9
  11.3 14.9 %all_gather.3 = bf16[128,2560]{1,0:T(8,128)(2,1)S(1)} all-gather(bf16[128,640]{1,0:T(8,128)(2,1)} %param.15), channel_id=1, replica_groups=mesh['dp'=32,'mp'=4] {'mp'}, dimensions={1}, use_global_device_ids=true | all-gather | bytes 819200 | tf_op jit(solution)/shard_map/all_gather | solution.py:57
  26.2 0.2 fusion.22
  26.5 0.7 convert_element_type.64
  27.2 1.6 convolution_convert_fusion.1
  28.8 0.0 copy-start.8
  28.8 69.5 %all_to_all.10 = bf16[32,2,16,2560]{3,2,1,0:T(8,128)(2,1)S(1)} all-to-all(bf16[32,2,16,2560]{3,2,1,0:T(8,128)(2,1)S(1)} %bitcast.98), channel_id=1, replica_groups=mesh['dp'=32,'mp'=4] {'dp'}, dimensions={0} | all-to-all | bytes 10485760 | tf_op jit(solution)/shard_map/all_to_all | solution.py:107
  98.3 0.0 copy-start.1
  98.3 2.3 copy-done.1
  100.6 0.0 copy-done.8
  100.6 2.9 fusion.3
  103.5 12.8 %fusion = bf16[32,2,16,2560]{3,2,0,1:T(8,128)(2,1)} fusion(bf16[2,384,2560]{2,1,0:T(8,128)(2,1)} %param.22, f32[2,32,16,384]{3,2,1,0:T(8,128)S(1)} %fusion.3, bf16[2,2560,384]{2,1,0:T(8,128)(2,1)} %param.21, bf16[32,2,16,2560]{3,2,1,0:T(8,128)(2,1)} %copy-done.1), kind=kOutput, calls=%fused_computation.2 | convolution fusion | flops 4031512576 | bytes 19922944 | tf_op jit(solution)/shard_map/sjcf,jfd->sjcd/dot_general | solution.py:13
  116.3 5.3 %copy.66 = bf16[32,2,16,2560]{3,2,1,0:T(8,128)(2,1)} copy(bf16[32,2,16,2560]{3,2,0,1:T(8,128)(2,1)} %fusion) | data formatting | bytes 10485760 | tf_op jit(solution)/shard_map/convert_element_type | solution.py:111
  121.5 0.0 copy-start.5
  121.5 5.0 %all-to-all-start.1 = ((bf16[32,2,16,2560]{3,2,1,0:T(8,128)(2,1)}), bf16[32,2,16,2560]{3,2,1,0:T(8,128)(2,1)}, u32[]{:S(2)}, u32[]{:S(2)}) async-start(bf16[32,2,16,2560]{3,2,1,0:T(8,128)(2,1)} %copy.66), calls=%async_computation.1 | async-start | bytes 10485760 | tf_op jit(solution)/shard_map/all_to_all | solution.py:105
  126.6 0.0 all-reduce.3.cloned.1.call-start
  126.6 0.0 copy-done.4
  126.6 0.0 copy-done.6
  126.6 0.4 fusion.25
  127.1 0.9 copy.95
  127.9 0.0 copy-done
  128.0 1.1 convolution_convert_fusion.3
  129.1 0.0 all-reduce.3.cloned.1.call-update
  129.1 0.2 reduce-scatter.4.cloned.1.call-start
  129.3 0.0 copy-done.7
  129.4 0.1 copy.67
  129.5 0.1 reduce-window.20
  129.5 0.1 reduce.1
  129.7 0.0 copy-start.9
  129.7 0.1 convert_reduce_fusion
  129.8 0.0 copy-done.10
  129.8 0.1 select_reduce_fusion.1
  129.9 0.0 copy-done.5
  129.9 0.4 select_reduce_fusion
  130.3 3.2 fusion.57
  133.5 0.0 copy-done.9
  133.5 0.0 copy-start.2
  133.5 0.8 fusion.26
  134.3 1.3 copy-done.2
  135.6 0.7 fusion.59
  136.3 131.0 %all-reduce.3.cloned.1.call-done = (bf16[16,16,640]{2,0,1:T(8,128)(2,1)}, bf16[16,16,768]{2,1,0:T(8,128)(2,1)}) async-done(((bf16[16,16,640]{2,0,1:T(8,128)(2,1)}, bf16[16,16,768]{2,1,0:T(8,128)(2,1)}), (bf16[16,16,640]{2,0,1:T(8,128)(2,1)}, bf16[16,16,768]{2,1,0:T(8,128)(2,1)})) %all-reduce.3.cloned.1.call-update) | async-done | bytes 720912 | tf_op jit(solution)/shard_map/psum | solution.py:56
  267.3 1.3 fusion.29
  268.6 10.8 %psum.22 = f32[128,16]{0,1:T(8,128)S(1)} all-reduce(f32[128,16]{0,1:T(8,128)S(1)} %fusion.29), channel_id=1, replica_groups=mesh['dp'=32,'mp'=4] {'mp'}, use_global_device_ids=true, to_apply=%region_11.12 | all-reduce | flops 2048 | bytes 16384 | tf_op jit(solution)/shard_map/psum | solution.py:82
  279.4 0.0 all-to-all-done.1
  279.4 3.3 %fusion.39 = f32[128,2560]{1,0:T(8,128)S(1)} fusion(bf16[1024,2560]{1,0:T(8,128)(2,1)} %bitcast.11, f32[128,1024]{1,0:T(8,128)S(1)} %select_reduce_fusion), kind=kOutput, calls=%fused_computation.53 | convolution fusion | flops 671219712 | bytes 7077888 | tf_op jit(solution)/shard_map/dot_general | solution.py:121
  282.7 0.0 copy-start.3
  282.7 3.5 %fusion.8 = f32[128,2560]{1,0:T(8,128)S(1)} fusion(f32[128,2560]{1,0:T(8,128)S(1)} %fusion.59, f32[128,2560]{1,0:T(8,128)S(1)} %fusion.39, bf16[1024,2560]{1,0:T(8,128)(2,1)} %bitcast.11, f32[128,1024]{1,0:T(8,128)S(1)} %select_reduce_fusion), kind=kOutput, calls=%fused_computation.11 | convolution fusion | flops 672268288 | bytes 9699328 | tf_op jit(solution)/shard_map/dot_general | solution.py:121
  286.2 0.0 copy-done.3
  286.2 0.4 fusion.28
  286.6 0.1 convert_element_type.80
  286.7 1.1 copy.75
  287.8 0.0 reduce-scatter.4.cloned.1.call-update
  287.8 19.6 %reduce-scatter.4.cloned.1.call-done = bf16[640,128]{1,0:T(8,128)(2,1)} async-done(((bf16[2560,128]{1,0:T(8,128)(2,1)}), bf16[640,128]{1,0:T(8,128)(2,1)}) %reduce-scatter.4.cloned.1.call-update) | async-done | bytes 163856
  307.4 1.7 copy.76
  (11 shorter events, 0.1 us)
Async XLA Ops:
  6.5 121.4 %copy-start = (bf16[2,16,2560]{2,1,0:T(8,128)(2,1)S(1)}, bf16[2,16,2560]{2,1,0:T(8,128)(2,1)}, u32[]{:S(2)}) copy-start(bf16[2,16,2560]{2,1,0:T(8,128)(2,1)} %param.24) | copy-start | bytes 491524
  28.8 71.8 %copy-start.8 = (bf16[2,2560,384]{2,1,0:T(8,128)(2,1)S(1)}, bf16[2,2560,384]{2,1,0:T(8,128)(2,1)}, u32[]{:S(2)}) copy-start(bf16[2,2560,384]{2,1,0:T(8,128)(2,1)} %param.20) | copy-start | bytes 11796484
  98.3 2.3 copy-start.1
  121.5 5.1 %copy-start.4 = (bf16[2,768,16]{1,2,0:T(8,128)(2,1)S(1)}, bf16[2,768,16]{1,2,0:T(8,128)(2,1)}, u32[]{:S(2)}) copy-start(bf16[2,768,16]{1,2,0:T(8,128)(2,1)} %param.23) | copy-start | bytes 147460
  121.5 5.1 %copy-start.6 = (s32[16]{0:T(128)S(1)}, s32[16]{0:T(128)}, u32[]{:S(2)}) copy-start(s32[16]{0:T(128)} %param.25) | copy-start | bytes 196
  121.5 7.8 %copy-start.7 = (s32[64]{0:T(128)S(1)}, s32[64]{0:T(128)}, u32[]{:S(2)}) copy-start(s32[64]{0:T(128)} %param.26) | copy-start | bytes 772
  121.5 8.2 %copy-start.10 = (s32[64]{0:T(128)S(1)}, s32[64]{0:T(128)}, u32[]{:S(2)}) copy-start(s32[64]{0:T(128)} %param.27) | copy-start | bytes 772
  121.5 8.3 %copy-start.5 = (f32[128,6]{0,1:T(8,128)S(1)}, f32[128,6]{0,1:T(8,128)}, u32[]{:S(2)}) copy-start(f32[128,6]{0,1:T(8,128)} %param.29) | copy-start | bytes 9220
  121.5 157.8 %all-to-all-start.1 = ((bf16[32,2,16,2560]{3,2,1,0:T(8,128)(2,1)}), bf16[32,2,16,2560]{3,2,1,0:T(8,128)(2,1)}, u32[]{:S(2)}, u32[]{:S(2)}) async-start(bf16[32,2,16,2560]{3,2,1,0:T(8,128)(2,1)} %copy.66), calls=%async_computation.1 | async-start | bytes 10485760 | tf_op jit(solution)/shard_map/all_to_all | solution.py:105
  126.6 140.7 %all-reduce.3.cloned.1.call-start = ((), (), s32[]{:S(2)}) async-start(), calls=%async_computation.4 | async-start | bytes 1441792 | tf_op jit(solution)/shard_map/psum | solution.py:56
  129.1 178.2 %reduce-scatter.4.cloned.1.call-start = ((), (), s32[]{:S(2)}) async-start(), calls=%async_computation.3 | async-start | bytes 819200
  129.7 3.8 %copy-start.9 = (bf16[2560,768]{1,0:T(8,128)(2,1)S(1)}, bf16[2560,768]{1,0:T(8,128)(2,1)}, u32[]{:S(2)}) copy-start(bf16[2560,768]{1,0:T(8,128)(2,1)} %param.18) | copy-start | bytes 11796484
  133.5 2.1 copy-start.2
  282.7 3.5 %copy-start.3 = (bf16[16,16,640]{2,0,1:T(8,128)(2,1)S(1)}, bf16[16,16,640]{2,0,1:T(8,128)(2,1)}, u32[]{:S(2)}) copy-start(bf16[16,16,640]{2,0,1:T(8,128)(2,1)} %get-tuple-element.5) | copy-start | bytes 983044
Sparse Core Ops, SparseCore 0:
  130.8 136.4 all-reduce.2
  287.9 19.4 reduce-scatter.3
where the time goes:
time: 316 us
  waiting for transfers between devices  151 us (48%)
  blocking collectives  95.2 us (30%)
  matrix products  31.9 us (10%)
  local copies, waits for them, and re-layouts  14.3 us (5%)
  between operations  13.7 us (4%)
  starting transfers between devices  5.27 us (2%)
  other arithmetic  4.99 us (2%)
    psum x1, waiting for transfers between devices, body(): picked_in, picked_out = lax.psum((picked_in, picked_out), 'dp')  131 us
    all_to_all x1, blocking collectives, body(): lax.all_to_all(send_rows, 'dp', split_axis=0, concat_axis=0, tiled=True)  69.5 us
    unnamed x3, waiting for transfers between devices  19.6 us
    all_gather x1, blocking collectives, body(): gathered = lax.all_gather(hidden, 'mp', axis=1, tiled=True)  14.9 us
    dot_general x1, matrix products, experts_apply(): jnp.einsum('sjcf,jfd->sjcd', inner, expert_down, preferred_element_type=j...  12.8 us
    psum x1, blocking collectives, body(): lowrank_sel = lax.psum(lowrank_sel, 'mp')  10.8 us
    unnamed x25, local copies, waits for them, and re-layouts  7.3 us
  transfers between devices with their start and end apart: 3, of which 2 were waited for; matrix products, arithmetic and copies ran while one was open for 3% of the time, Pallas kernels for 0%

commit v1 on v0

--- a/solution.py
+++ b/solution.py
@@ -2,6 +2,10 @@
 import jax.numpy as jnp
 from jax import lax
 from jax.sharding import PartitionSpec as P
+
+
+def change_roots(a0):
+    return jnp.sum(lax.all_gather(a0, "mp"), 0)
 
 
 def experts_apply(slots_in, expert_gate, expert_up, expert_down):
@@ -79,7 +83,7 @@
     lowrank_sel = jnp.sum(
         lowrank.reshape(tok_rows, active_count, rank_width) * chosen[:, :, None], axis=1
     )
-    lowrank_sel = lax.psum(lowrank_sel, "mp")
+    lowrank_sel = change_roots(lowrank_sel)
     lowrank = (chosen[:, :, None] * lowrank_sel[:, None, :]).reshape(
         tok_rows, active_count * rank_width
     )

time: 316 us -> 320 us (1.013)
    all_gather x0 -> x1, blocking collectives: none -> 12.4 us  [change_roots(): return jnp.sum(lax.all_gather(a0, 'mp'), 0)]
    psum x1 -> x0, blocking collectives: 10.8 us -> none  [body(): lowrank_sel = lax.psum(lowrank_sel, 'mp')]
where the time goes in v1:
time: 320 us; the launch traced here: 319 us
  waiting for transfers between devices  152 us (48%)
  blocking collectives  96.8 us (30%)
  matrix products  31.9 us (10%)
  local copies, waits for them, and re-layouts  14.3 us (4%)
  between operations  13.7 us (4%)
  starting transfers between devices  5.27 us (2%)
  other arithmetic  5.01 us (2%)
    psum x1, waiting for transfers between devices, body(): picked_in, picked_out = lax.psum((picked_in, picked_out), 'dp')  131 us
    all_to_all x1, blocking collectives, body(): lax.all_to_all(send_rows, 'dp', split_axis=0, concat_axis=0, tiled=True)  69.5 us
    unnamed x3, waiting for transfers between devices  21.3 us
    all_gather x1, blocking collectives, body(): gathered = lax.all_gather(hidden, 'mp', axis=1, tiled=True)  14.9 us
    dot_general x1, matrix products, experts_apply(): jnp.einsum('sjcf,jfd->sjcd', inner, expert_down, preferred_element_type=j...  12.8 us
    all_gather x1, blocking collectives, change_roots(): return jnp.sum(lax.all_gather(a0, 'mp'), 0)  12.4 us
    unnamed x25, local copies, waits for them, and re-layouts  7.3 us
  transfers between devices with their start and end apart: 3, of which 2 were waited for; matrix products, arithmetic and copies ran while one was open for 3% of the time, Pallas kernels for 0%

profile of v1, /device:TPU:0, one launch (start us, length us, event | category | flops | bytes accessed | tf_op | source)
XLA Modules:
  0.0 319.2 jit_solution(14107938899039969940)
XLA Ops:
  6.5 0.0 copy-start
  6.5 0.8 copy.60
  7.4 0.1 eq.85
  7.5 0.1 eq.81
  7.7 1.8 reduce-window.18
  9.5 0.3 slice_reduce_fusion
  9.8 0.1 fusion.34
  9.9 0.1 reduce_sum.67
  10.1 0.1 copy.63
  10.1 0.7 multiply_add_fusion
  10.8 0.5 fusion.9
  11.3 14.9 %all_gather.9 = bf16[128,2560]{1,0:T(8,128)(2,1)S(1)} all-gather(bf16[128,640]{1,0:T(8,128)(2,1)} %param.15), channel_id=1, replica_groups=mesh['dp'=32,'mp'=4] {'mp'}, dimensions={1}, use_global_device_ids=true | all-gather | bytes 819200 | tf_op jit(solution)/shard_map/all_gather | solution.py:61
  26.2 0.2 fusion.22
  26.5 0.7 convert_element_type.64
  27.2 1.6 convolution_convert_fusion.1
  28.8 0.0 copy-start.8
  28.8 69.5 %all_to_all.10 = bf16[32,2,16,2560]{3,2,1,0:T(8,128)(2,1)S(1)} all-to-all(bf16[32,2,16,2560]{3,2,1,0:T(8,128)(2,1)S(1)} %bitcast.100), channel_id=1, replica_groups=mesh['dp'=32,'mp'=4] {'dp'}, dimensions={0} | all-to-all | bytes 10485760 | tf_op jit(solution)/shard_map/all_to_all | solution.py:111
  98.3 0.0 copy-start.1
  98.3 2.3 copy-done.1
  100.6 0.0 copy-done.8
  100.6 2.9 fusion.3
  103.5 12.8 %fusion = bf16[32,2,16,2560]{3,2,0,1:T(8,128)(2,1)} fusion(bf16[2,384,2560]{2,1,0:T(8,128)(2,1)} %param.22, f32[2,32,16,384]{3,2,1,0:T(8,128)S(1)} %fusion.3, bf16[2,2560,384]{2,1,0:T(8,128)(2,1)} %param.21, bf16[32,2,16,2560]{3,2,1,0:T(8,128)(2,1)} %copy-done.1), kind=kOutput, calls=%fused_computation.2 | convolution fusion | flops 4031512576 | bytes 19922944 | tf_op jit(solution)/shard_map/sjcf,jfd->sjcd/dot_general | solution.py:17
  116.3 5.3 %copy.66 = bf16[32,2,16,2560]{3,2,1,0:T(8,128)(2,1)} copy(bf16[32,2,16,2560]{3,2,0,1:T(8,128)(2,1)} %fusion) | data formatting | bytes 10485760 | tf_op jit(solution)/shard_map/convert_element_type | solution.py:115
  121.5 0.0 copy-start.5
  121.5 5.0 %all-to-all-start.1 = ((bf16[32,2,16,2560]{3,2,1,0:T(8,128)(2,1)}), bf16[32,2,16,2560]{3,2,1,0:T(8,128)(2,1)}, u32[]{:S(2)}, u32[]{:S(2)}) async-start(bf16[32,2,16,2560]{3,2,1,0:T(8,128)(2,1)} %copy.66), calls=%async_computation.1 | async-start | bytes 10485760 | tf_op jit(solution)/shard_map/all_to_all | solution.py:109
  126.6 0.0 all-reduce.3.cloned.1.call-start
  126.6 0.0 copy-done.4
  126.6 0.0 copy-done.6
  126.6 0.4 fusion.25
  127.1 0.9 copy.95
  127.9 0.0 copy-done
  128.0 1.1 convolution_convert_fusion.3
  129.1 0.0 all-reduce.3.cloned.1.call-update
  129.1 0.2 reduce-scatter.4.cloned.1.call-start
  129.3 0.0 copy-done.7
  129.4 0.1 copy.67
  129.5 0.1 reduce-window.20
  129.5 0.1 reduce.1
  129.7 0.0 copy-start.9
  129.7 0.1 convert_reduce_fusion
  129.8 0.0 copy-done.10
  129.8 0.1 select_reduce_fusion.1
  129.9 0.0 copy-done.5
  129.9 0.4 select_reduce_fusion
  130.3 3.2 fusion.57
  133.5 0.0 copy-done.9
  133.5 0.0 copy-start.2
  133.5 0.8 fusion.26
  134.3 1.3 copy-done.2
  135.6 0.7 fusion.59
  136.3 131.0 %all-reduce.3.cloned.1.call-done = (bf16[16,16,640]{2,0,1:T(8,128)(2,1)}, bf16[16,16,768]{2,1,0:T(8,128)(2,1)}) async-done(((bf16[16,16,640]{2,0,1:T(8,128)(2,1)}, bf16[16,16,768]{2,1,0:T(8,128)(2,1)}), (bf16[16,16,640]{2,0,1:T(8,128)(2,1)}, bf16[16,16,768]{2,1,0:T(8,128)(2,1)})) %all-reduce.3.cloned.1.call-update) | async-done | bytes 720912 | tf_op jit(solution)/shard_map/psum | solution.py:60
  267.3 1.3 fusion.29
  268.6 12.4 %all-gather = f32[512,16]{0,1:T(8,128)S(1)} all-gather(f32[128,16]{0,1:T(8,128)S(1)} %fusion.29), channel_id=2, replica_groups=mesh['dp'=32,'mp'=4] {'mp'}, dimensions={0}, use_global_device_ids=true | all-gather | bytes 40960 | tf_op jit(solution)/shard_map/all_gather | solution.py:8
  281.0 0.0 all-to-all-done.1
  281.0 3.3 %fusion.39 = f32[128,2560]{1,0:T(8,128)S(1)} fusion(bf16[1024,2560]{1,0:T(8,128)(2,1)} %bitcast.11, f32[128,1024]{1,0:T(8,128)S(1)} %select_reduce_fusion), kind=kOutput, calls=%fused_computation.53 | convolution fusion | flops 671219712 | bytes 7077888 | tf_op jit(solution)/shard_map/dot_general | solution.py:125
  284.4 0.0 copy-start.3
  284.4 3.5 %fusion.8 = f32[128,2560]{1,0:T(8,128)S(1)} fusion(f32[128,2560]{1,0:T(8,128)S(1)} %fusion.59, f32[128,2560]{1,0:T(8,128)S(1)} %fusion.39, bf16[1024,2560]{1,0:T(8,128)(2,1)} %bitcast.11, f32[128,1024]{1,0:T(8,128)S(1)} %select_reduce_fusion), kind=kOutput, calls=%fused_computation.11 | convolution fusion | flops 672268288 | bytes 9699328 | tf_op jit(solution)/shard_map/dot_general | solution.py:125
  287.9 0.0 copy-done.3
  287.9 0.4 fusion.28
  288.2 0.1 convert_element_type.80
  288.3 1.1 copy.75
  289.4 0.0 reduce-scatter.4.cloned.1.call-update
  289.4 21.3 %reduce-scatter.4.cloned.1.call-done = bf16[640,128]{1,0:T(8,128)(2,1)} async-done(((bf16[2560,128]{1,0:T(8,128)(2,1)}), bf16[640,128]{1,0:T(8,128)(2,1)}) %reduce-scatter.4.cloned.1.call-update) | async-done | bytes 163856
  310.7 1.7 copy.76
  (13 shorter events, 0.1 us)
Async XLA Ops:
  6.5 121.4 %copy-start = (bf16[2,16,2560]{2,1,0:T(8,128)(2,1)S(1)}, bf16[2,16,2560]{2,1,0:T(8,128)(2,1)}, u32[]{:S(2)}) copy-start(bf16[2,16,2560]{2,1,0:T(8,128)(2,1)} %param.24) | copy-start | bytes 491524
  28.8 71.8 %copy-start.8 = (bf16[2,2560,384]{2,1,0:T(8,128)(2,1)S(1)}, bf16[2,2560,384]{2,1,0:T(8,128)(2,1)}, u32[]{:S(2)}) copy-start(bf16[2,2560,384]{2,1,0:T(8,128)(2,1)} %param.20) | copy-start | bytes 11796484
  98.3 2.3 copy-start.1
  121.5 5.1 %copy-start.4 = (bf16[2,768,16]{1,2,0:T(8,128)(2,1)S(1)}, bf16[2,768,16]{1,2,0:T(8,128)(2,1)}, u32[]{:S(2)}) copy-start(bf16[2,768,16]{1,2,0:T(8,128)(2,1)} %param.23) | copy-start | bytes 147460
  121.5 5.1 %copy-start.6 = (s32[16]{0:T(128)S(1)}, s32[16]{0:T(128)}, u32[]{:S(2)}) copy-start(s32[16]{0:T(128)} %param.25) | copy-start | bytes 196
  121.5 7.8 %copy-start.7 = (s32[64]{0:T(128)S(1)}, s32[64]{0:T(128)}, u32[]{:S(2)}) copy-start(s32[64]{0:T(128)} %param.26) | copy-start | bytes 772
  121.5 8.2 %copy-start.10 = (s32[64]{0:T(128)S(1)}, s32[64]{0:T(128)}, u32[]{:S(2)}) copy-start(s32[64]{0:T(128)} %param.27) | copy-start | bytes 772
  121.5 8.3 %copy-start.5 = (f32[128,6]{0,1:T(8,128)S(1)}, f32[128,6]{0,1:T(8,128)}, u32[]{:S(2)}) copy-start(f32[128,6]{0,1:T(8,128)} %param.29) | copy-start | bytes 9220
  121.5 159.5 %all-to-all-start.1 = ((bf16[32,2,16,2560]{3,2,1,0:T(8,128)(2,1)}), bf16[32,2,16,2560]{3,2,1,0:T(8,128)(2,1)}, u32[]{:S(2)}, u32[]{:S(2)}) async-start(bf16[32,2,16,2560]{3,2,1,0:T(8,128)(2,1)} %copy.66), calls=%async_computation.1 | async-start | bytes 10485760 | tf_op jit(solution)/shard_map/all_to_all | solution.py:109
  126.6 140.7 %all-reduce.3.cloned.1.call-start = ((), (), s32[]{:S(2)}) async-start(), calls=%async_computation.4 | async-start | bytes 1441792 | tf_op jit(solution)/shard_map/psum | solution.py:60
  129.1 181.6 %reduce-scatter.4.cloned.1.call-start = ((), (), s32[]{:S(2)}) async-start(), calls=%async_computation.3 | async-start | bytes 819200
  129.7 3.8 %copy-start.9 = (bf16[2560,768]{1,0:T(8,128)(2,1)S(1)}, bf16[2560,768]{1,0:T(8,128)(2,1)}, u32[]{:S(2)}) copy-start(bf16[2560,768]{1,0:T(8,128)(2,1)} %param.18) | copy-start | bytes 11796484
  133.5 2.1 copy-start.2
  284.4 3.5 %copy-start.3 = (bf16[16,16,640]{2,0,1:T(8,128)(2,1)S(1)}, bf16[16,16,640]{2,0,1:T(8,128)(2,1)}, u32[]{:S(2)}) copy-start(bf16[16,16,640]{2,0,1:T(8,128)(2,1)} %get-tuple-element.5) | copy-start | bytes 983044
Sparse Core Ops, SparseCore 0:
  130.8 136.4 all-reduce.2
  289.5 21.0 reduce-scatter.3
